TPU v7x, 128 devices: a whole 4x4x4 slice. The times are simulated.
128 devices in a mesh: dp: 32 (over z, y, core), mp: 4 (over x).
Axes of the slice: x: 4, y: 4, z: 4, core: 2. Of those that a mesh axis runs over, the one named last changes fastest.
Arguments:
- tokens: bfloat16 [57344, 1024], P('dp'), may hold values from -60 to 60
- segment_ids: int32 [57344], P('dp'), may hold values from 0 to 127, as said below
- page_table: int32 [448], P('dp'), may hold values from 0 to 447, as said below
- w_query: bfloat16 [1024, 1024], P('dp', 'mp'), may hold values from -0.1875 to 0.1875
- w_key: bfloat16 [1024, 1024], P('dp', 'mp'), may hold values from -0.1875 to 0.1875
- w_value: bfloat16 [1024, 1024], P('dp', 'mp'), may hold values from -0.1875 to 0.1875
- w_out: bfloat16 [1024, 1024], P('mp', 'dp'), may hold values from -1.5 to 1.5
- w_up: bfloat16 [1024, 4096], P('dp', 'mp'), may hold values from -0.1875 to 0.1875
- w_down: bfloat16 [4096, 1024], P('mp', 'dp'), may hold values from -0.09375 to 0.09375
- gain_first: float32 [1024], replicated, may hold values from 0.1 to 1.9
- shift_first: float32 [1024], replicated, may hold values from -3 to 3
- gain_second: float32 [1024], replicated, may hold values from 0.1 to 1.9
- shift_second: float32 [1024], replicated, may hold values from -3 to 3
Outputs:
- mixed: bfloat16 [57344, 1024], P('dp')
- kv_cache: bfloat16 [57344, 2, 1024], P('dp', None, 'mp')
Inputs may be any that keep to these rules, and one draw needn't show every extreme that they name: page_table is a permutation of the page slots. Page p lies on device p // 14 in arrival order and goes to device page_table[p] // 14; from one device at most 1 pages go to one device, and some pair reaches 1. `segment_ids`: tokens with equal ids form one request; after dealing, a request's tokens are consecutive and lie on one device, which holds at most 4 requests.
All inputs are finite; a program needn't handle non-finite values.
Results may differ from a plain program's by a relative error of at most 0.014.
Values may be sent and summed in bfloat16 or wider, within the bound.
No kernel may reach another device: no remote copies, remote signals or barrier semaphores. Data moves between devices by JAX's collectives and lax.ppermute only.
A program may use at most 128 MiB of HBM per device.

v0:
```python
import jax
import jax.numpy as jnp
from jax import lax
from jax.sharding import PartitionSpec as P

HEAD = 64


def layer_norm(hidden_sum, gain, shift):
    center = hidden_sum - jnp.mean(hidden_sum, axis=-1, keepdims=True)
    spread = jnp.mean(center * center, axis=-1, keepdims=True)
    return center * lax.rsqrt(spread + 1e-05) * gain + shift


def attend_head(query, keys, values, segments, block_rows):
    blocks = query.shape[0] // block_rows
    query_blocks = query.reshape(blocks, block_rows, query.shape[1])
    segment_blocks = segments.reshape(blocks, block_rows)

    def per_block(bundle):
        rows, row_ids = bundle
        scores = jnp.einsum("qd,kd->qk", rows, keys, preferred_element_type=jnp.float32) * HEAD ** (
            -0.5
        )
        scores = jnp.where(row_ids[:, None] == segments[None, :], scores, -1e30)
        highest = jnp.max(scores, axis=1, keepdims=True)
        raised = jnp.exp(scores - highest)
        attn_weights = (raised / jnp.sum(raised, axis=1, keepdims=True)).astype(jnp.bfloat16)
        return jnp.dot(attn_weights, values, preferred_element_type=jnp.float32).astype(
            jnp.bfloat16
        )

    return lax.map(per_block, (query_blocks, segment_blocks)).reshape(
        query.shape[0], values.shape[1]
    )


def body(
    tokens,
    segment_ids,
    page_table,
    w_query,
    w_key,
    w_value,
    w_out,
    w_up,
    w_down,
    gain_first,
    shift_first,
    gain_second,
    shift_second,
):
    n_data = lax.axis_size("dp")
    n_model = lax.axis_size("mp")
    me_model = lax.axis_index("mp")
    pages_dev = page_table.shape[0]
    page = tokens.shape[0] // pages_dev
    width = tokens.shape[1]
    quarter = width // n_model
    sub = page // n_model
    slots_per = (pages_dev + n_data - 1) // n_data
    buffer_rows = n_data * slots_per
    head_cols = w_query.shape[1]
    unit_cols = w_up.shape[1]
    local = jnp.concatenate([w_query, w_key, w_value, w_up, w_out.T, w_down.T], axis=1)
    gathered = lax.all_gather(local, "dp", axis=0, tiled=True)
    at = 0
    full_query = gathered[:, at : at + head_cols]
    at += head_cols
    full_key = gathered[:, at : at + head_cols]
    at += head_cols
    full_value = gathered[:, at : at + head_cols]
    at += head_cols
    full_up = gathered[:, at : at + unit_cols]
    at += unit_cols
    out_t = gathered[:, at : at + w_out.shape[0]]
    at += w_out.shape[0]
    down_t = gathered[:, at : at + w_down.shape[0]]
    out_all_t = lax.all_gather(out_t, "mp", axis=1, tiled=True)
    target = page_table // pages_dev
    local_slot = page_table % pages_dev
    order = jnp.arange(pages_dev, dtype=jnp.int32)
    earlier = (target[:, None] == target[None, :]) & (order[:, None] < order[None, :])
    rank = jnp.sum(earlier.astype(jnp.int32), axis=0)
    position = target * slots_per + rank
    meta = jnp.concatenate([segment_ids.reshape(pages_dev, page), local_slot[:, None]], axis=1)
    send_meta = (
        jnp.zeros((buffer_rows, page + 1), jnp.int32).at[:, page].set(-1).at[position].set(meta)
    )
    token_part = lax.dynamic_slice_in_dim(tokens, me_model * quarter, quarter, axis=1)
    send_pages = (
        jnp.zeros((buffer_rows, page, quarter), tokens.dtype)
        .at[position]
        .set(token_part.reshape(pages_dev, page, quarter))
    )
    got_pages = lax.all_to_all(send_pages, "dp", split_axis=0, concat_axis=0, tiled=True)
    got_meta = lax.all_to_all(send_meta, "dp", split_axis=0, concat_axis=0, tiled=True)
    got_ids = got_meta[:, :page]
    got_slots = got_meta[:, page]
    matches = got_slots[None, :] == order[:, None]
    source_row = jnp.sum(
        jnp.where(matches, jnp.arange(buffer_rows, dtype=jnp.int32)[None, :], 0), axis=1
    )
    dealt_part = got_pages[source_row]
    dealt = lax.all_gather(dealt_part, "mp", axis=2, tiled=True).reshape(pages_dev * page, width)
    dealt_ids = got_ids[source_row].reshape(pages_dev * page)
    query = jnp.dot(dealt, full_query, preferred_element_type=jnp.float32).astype(jnp.bfloat16)
    keys = jnp.dot(dealt, full_key, preferred_element_type=jnp.float32).astype(jnp.bfloat16)
    values = jnp.dot(dealt, full_value, preferred_element_type=jnp.float32).astype(jnp.bfloat16)
    suitable = [
        count for count in range(1, pages_dev + 1) if pages_dev % count == 0 and count * page >= 512
    ]
    block_rows = suitable[0] * page
    heads_here = query.shape[1] // HEAD
    contexts = []
    for head in range(heads_here):
        cols = slice(head * HEAD, (head + 1) * HEAD)
        contexts.append(
            attend_head(query[:, cols], keys[:, cols], values[:, cols], dealt_ids, block_rows)
        )
    context = jnp.concatenate(contexts, axis=1)
    context_rows = lax.all_to_all(
        context.reshape(pages_dev, n_model, sub, head_cols),
        "mp",
        split_axis=1,
        concat_axis=1,
        tiled=True,
    )
    attended = jnp.zeros((pages_dev, sub, width), jnp.float32)
    for group in range(n_model):
        term = jnp.einsum(
            "pic,oc->pio",
            context_rows[:, group],
            out_all_t[:, group * head_cols : (group + 1) * head_cols],
            preferred_element_type=jnp.float32,
        ).astype(jnp.bfloat16)
        attended = attended + term.astype(jnp.float32)
    dealt_mine = lax.dynamic_index_in_dim(
        dealt.reshape(pages_dev, n_model, sub, width), me_model, axis=1, keepdims=False
    )
    first_mine = layer_norm(
        dealt_mine.astype(jnp.float32) + attended, gain_first, shift_first
    ).astype(jnp.bfloat16)
    first = lax.all_gather(first_mine, "mp", axis=1).reshape(pages_dev * page, width)
    hidden = jax.nn.gelu(
        jnp.dot(first, full_up, preferred_element_type=jnp.float32), approximate=False
    ).astype(jnp.bfloat16)
    fed_term = jnp.einsum("tu,ou->to", hidden, down_t, preferred_element_type=jnp.float32).astype(
        jnp.bfloat16
    )
    fed = lax.psum_scatter(
        fed_term.reshape(pages_dev, n_model, sub, width), "mp", scatter_dimension=1, tiled=True
    ).reshape(pages_dev, sub, width)
    second_mine = layer_norm(
        first_mine.astype(jnp.float32) + fed.astype(jnp.float32), gain_second, shift_second
    ).astype(jnp.bfloat16)
    valid = got_slots >= 0
    outgoing = jnp.where(
        valid[:, None, None],
        second_mine[jnp.clip(got_slots, 0, pages_dev - 1)],
        jnp.zeros((), second_mine.dtype),
    )
    returned = lax.all_to_all(outgoing, "dp", split_axis=0, concat_axis=0, tiled=True)
    mixed_mine = returned[position]
    mixed = lax.all_gather(mixed_mine, "mp", axis=1).reshape(pages_dev * page, width)
    kv_cache = jnp.stack([keys, values], axis=1)
    return (mixed, kv_cache)


def solution(mesh):
    return jax.shard_map(
        body,
        mesh=mesh,
        in_specs=(
            P("dp", None),
            P("dp"),
            P("dp"),
            P("dp", "mp"),
            P("dp", "mp"),
            P("dp", "mp"),
            P("mp", "dp"),
            P("dp", "mp"),
            P("mp", "dp"),
            P(),
            P(),
            P(),
            P(),
        ),
        out_specs=(P("dp", None), P("dp", None, "mp")),
        check_vma=False,
    )
```

profile of v0, /device:TPU:1, one launch (start us, length us, event | category | flops | bytes accessed | tf_op | source)
XLA Modules:
  0.0 474.3 jit_solution(7659568354544722614)
XLA Ops:
  10.2 9.6 %all-to-all-start = ((s32[32,1,129]{2,1,0:T(1,128)}), s32[32,1,129]{2,1,0:T(1,128)S(1)}, u32[]{:S(2)}, u32[]{:S(2)}) async-start(s32[32,1,129]{2,1,0:T(1,128)} %all_to_all.17), calls=%async_computation | async-start | bytes 65536 | tf_op jit(solution)/shard_map/all_to_all | solution.py:97
  27.1 5.9 %all-to-all-start.1 = ((bf16[32,128,256]{2,1,0:T(8,128)(2,1)}), bf16[32,128,256]{2,1,0:T(8,128)(2,1)S(1)}, u32[]{:S(2)}, u32[]{:S(2)}) async-start(bf16[32,128,256]{2,1,0:T(8,128)(2,1)} %scatter_fusion), calls=%async_computation.1 | async-start | bytes 4194304 | tf_op jit(solution)/shard_map/all_to_all | solution.py:96
  34.2 27.3 %all-to-all-done.1 = bf16[32,128,256]{2,1,0:T(8,128)(2,1)S(1)} async-done(((bf16[32,128,256]{2,1,0:T(8,128)(2,1)}), bf16[32,128,256]{2,1,0:T(8,128)(2,1)S(1)}, u32[]{:S(2)}, u32[]{:S(2)}) %all-to-all-start.1) | async-done | bytes 2097184 | tf_op jit(solution)/shard_map/all_to_all | solution.py:96
  64.6 42.6 %all-gather.13.cloned.1.call-done = bf16[14,128,1024]{2,1,0:T(8,128)(2,1)} async-done(((bf16[14,128,256]{2,1,0:T(8,128)(2,1)}), bf16[14,128,1024]{2,1,0:T(8,128)(2,1)}) %all-gather.13.cloned.1.call-update) | async-done | bytes 3670032 | tf_op jit(solution)/shard_map/all_gather | solution.py:105
  107.2 54.7 %all-gather.9.cloned.1.call-done = bf16[1024,3072]{1,0:T(8,128)(2,1)} async-done(((bf16[32,3072]{1,0:T(8,128)(2,1)}), bf16[1024,3072]{1,0:T(8,128)(2,1)}) %all-gather.9.cloned.1.call-update) | async-done | bytes 6291472 | tf_op jit(solution)/shard_map/all_gather | solution.py:66
  162.0 3.3 convolution_convert_fusion.2
  167.2 3.3 convolution_convert_fusion.1
  172.6 3.3 convolution_convert_fusion.3
  176.9 8.2 %while.41 = (s32[]{:T(128)}, bf16[2,896,64]{1,2,0:T(8,128)(2,1)S(1)}, s32[2,896]{1,0:T(2,128)S(1)}, s32[14,128]{1,0:T(8,128)S(1)}, bf16[2,896,64]{2,1,0:T(8,128)...) while((s32[]{:T(128)}, bf16[2,896,64]{1,2,0:T(8,128)(2,1)S(1)}, ...), condition=%wide.region_7.8_spmd, body=%wide.region_4.7_spmd.sunk | while | flops 425548032 | bytes 20567648 | solution.py:33
  187.0 7.7 %while.42 = (s32[]{:T(128)}, bf16[2,896,64]{1,2,0:T(8,128)(2,1)S(1)}, s32[2,896]{1,0:T(2,128)S(1)}, s32[14,128]{1,0:T(8,128)S(1)}, bf16[2,896,64]{2,1,0:T(8,128)...) while((s32[]{:T(128)}, bf16[2,896,64]{1,2,0:T(8,128)(2,1)S(1)}, ...), condition=%wide.region_11.12_spmd, body=%wide.region_8.11_spmd.sunk | while | flops 425548032 | bytes 20567648 | solution.py:33
  195.8 7.8 %while.43 = (s32[]{:T(128)}, bf16[2,896,64]{1,2,0:T(8,128)(2,1)S(1)}, s32[2,896]{1,0:T(2,128)S(1)}, s32[14,128]{1,0:T(8,128)S(1)}, bf16[2,896,64]{2,1,0:T(8,128)...) while((s32[]{:T(128)}, bf16[2,896,64]{1,2,0:T(8,128)(2,1)S(1)}, ...), condition=%wide.region_15.16_spmd, body=%wide.region_12.15_spmd.sunk | while | flops 425548032 | bytes 20567648 | solution.py:33
  206.7 7.7 %while.44 = (s32[]{:T(128)}, bf16[2,896,64]{1,2,0:T(8,128)(2,1)S(1)}, s32[2,896]{1,0:T(2,128)S(1)}, s32[14,128]{1,0:T(8,128)S(1)}, bf16[2,896,64]{2,1,0:T(8,128)...) while((s32[]{:T(128)}, bf16[2,896,64]{1,2,0:T(8,128)(2,1)S(1)}, ...), condition=%wide.region_19.20_spmd, body=%wide.region_16.19_spmd.sunk | while | flops 425548032 | bytes 20567648 | solution.py:33
  216.3 4.0 all-to-all-start.2
  220.2 19.1 %all-to-all-done.2 = bf16[14,4,32,256]{3,2,0,1:T(8,128)(2,1)S(1)} async-done(((bf16[14,4,32,256]{3,2,0,1:T(8,128)(2,1)}), bf16[14,4,32,256]{3,2,0,1:T(8,128)(2,1)S(1)}, u32[]{:S(2)}, u32[]{:S(2)}) %all-to-all-start.2) | async-done | bytes 917536 | tf_op jit(solution)/shard_map/all_to_all | solution.py:122
  239.3 6.3 %all-gather.11.cloned.1.call-done = bf16[1024,1024]{1,0:T(8,128)(2,1)} async-done(((bf16[1024,256]{1,0:T(8,128)(2,1)}), bf16[1024,1024]{1,0:T(8,128)(2,1)}) %all-gather.11.cloned.1.call-update) | async-done | bytes 2097168 | tf_op jit(solution)/shard_map/all_gather | solution.py:79
  254.0 44.9 %all-gather.15.cloned.1.call-done = bf16[14,128,1024]{2,1,0:T(8,128)(2,1)} async-done(((bf16[14,32,1024]{2,1,0:T(8,128)(2,1)}), bf16[14,128,1024]{2,1,0:T(8,128)(2,1)}) %all-gather.15.cloned.1.call-update) | async-done | bytes 3670032 | tf_op jit(solution)/shard_map/all_gather | solution.py:144
  298.9 26.1 %convolution_convert_fusion = bf16[1792,1024]{1,0:T(8,128)(2,1)} fusion(bf16[1024,3072]{1,0:T(8,128)(2,1)} %all-gather.9.cloned.1.call-done, bf16[1792,1024]{1,0:T(8,128)(2,1)} %bitcast.184), kind=kOutput, calls=%fused_computation.73 | convolution fusion | flops 7637303296 | bytes 11534336 | tf_op jit(solution)/shard_map/tu,ou->to/dot_general | solution.py:148
  325.0 4.5 copy.99
  329.6 43.0 %reduce-scatter.2.cloned.1.call-done = bf16[14,1,32,1024]{3,2,0,1:T(8,128)(2,1)} async-done(((bf16[14,4,32,1024]{3,2,0,1:T(8,128)(2,1)}), bf16[14,1,32,1024]{3,2,0,1:T(8,128)(2,1)}) %reduce-scatter.2.cloned.1.call-update) | async-done | bytes 917520 | tf_op jit(solution)/shard_map/reduce_scatter | solution.py:151
  384.4 7.8 %all-to-all-start.3 = ((bf16[32,32,1024]{2,1,0:T(8,128)(2,1)}), bf16[32,32,1024]{2,1,0:T(8,128)(2,1)S(1)}, u32[]{:S(2)}, u32[]{:S(2)}) async-start(bf16[32,32,1024]{2,1,0:T(8,128)(2,1)} %broadcast_select_fusion), calls=%async_computation.4 | async-start | bytes 4194304 | tf_op jit(solution)/shard_map/all_to_all | solution.py:163
  392.3 28.5 %all-to-all-done.3 = bf16[32,32,1024]{2,1,0:T(8,128)(2,1)S(1)} async-done(((bf16[32,32,1024]{2,1,0:T(8,128)(2,1)}), bf16[32,32,1024]{2,1,0:T(8,128)(2,1)S(1)}, u32[]{:S(2)}, u32[]{:S(2)}) %all-to-all-start.3) | async-done | bytes 2097184 | tf_op jit(solution)/shard_map/all_to_all | solution.py:163
  423.7 3.6 copy.100
  427.3 35.7 %all-gather.17.cloned.1.call-done = bf16[14,128,1024]{2,1,0:T(8,128)(2,1)} async-done(((bf16[14,32,1024]{2,1,0:T(8,128)(2,1)}), bf16[14,128,1024]{2,1,0:T(8,128)(2,1)}) %all-gather.17.cloned.1.call-update) | async-done | bytes 3670032 | tf_op jit(solution)/shard_map/all_gather | solution.py:165
  463.0 4.2 copy.146
  (162 shorter events, 80.7 us)
Async XLA Ops:
  7.9 19.1 %copy-start.18 = (s32[14]{0:T(128)}, s32[14]{0:T(128)S(1)}, u32[]{:S(2)}) copy-start(s32[14]{0:T(128)S(1)} %compare_select_fusion.2) | copy-start | bytes 172
  10.2 16.9 %all-to-all-start = ((s32[32,1,129]{2,1,0:T(1,128)}), s32[32,1,129]{2,1,0:T(1,128)S(1)}, u32[]{:S(2)}, u32[]{:S(2)}) async-start(s32[32,1,129]{2,1,0:T(1,128)} %all_to_all.17), calls=%async_computation | async-start | bytes 65536 | tf_op jit(solution)/shard_map/all_to_all | solution.py:97
  21.1 42.1 %copy-start.12 = (bf16[32,256]{1,0:T(8,128)(2,1)S(1)}, bf16[32,256]{1,0:T(8,128)(2,1)}, u32[]{:S(2)}) copy-start(bf16[32,256]{1,0:T(8,128)(2,1)} %param.26) | copy-start | bytes 49156
  21.1 42.1 %copy-start.13 = (bf16[32,256]{1,0:T(8,128)(2,1)S(1)}, bf16[32,256]{1,0:T(8,128)(2,1)}, u32[]{:S(2)}) copy-start(bf16[32,256]{1,0:T(8,128)(2,1)} %param.27) | copy-start | bytes 49156
  21.1 42.1 %copy-start.14 = (bf16[32,256]{1,0:T(8,128)(2,1)S(1)}, bf16[32,256]{1,0:T(8,128)(2,1)}, u32[]{:S(2)}) copy-start(bf16[32,256]{1,0:T(8,128)(2,1)} %param.28) | copy-start | bytes 49156
  21.1 42.1 %copy-start.10 = (bf16[32,1024]{1,0:T(8,128)(2,1)S(1)}, bf16[32,1024]{1,0:T(8,128)(2,1)}, u32[]{:S(2)}) copy-start(bf16[32,1024]{1,0:T(8,128)(2,1)} %param.30) | copy-start | bytes 196612
  21.1 42.1 %copy-start.15 = (bf16[256,32]{0,1:T(8,128)(2,1)S(1)}, bf16[256,32]{0,1:T(8,128)(2,1)}, u32[]{:S(2)}) copy-start(bf16[256,32]{0,1:T(8,128)(2,1)} %param.29) | copy-start | bytes 49156
  21.1 42.1 %copy-start.11 = (bf16[1024,32]{0,1:T(8,128)(2,1)S(1)}, bf16[1024,32]{0,1:T(8,128)(2,1)}, u32[]{:S(2)}) copy-start(bf16[1024,32]{0,1:T(8,128)(2,1)} %param.31) | copy-start | bytes 196612
  27.1 34.5 %all-to-all-start.1 = ((bf16[32,128,256]{2,1,0:T(8,128)(2,1)}), bf16[32,128,256]{2,1,0:T(8,128)(2,1)S(1)}, u32[]{:S(2)}, u32[]{:S(2)}) async-start(bf16[32,128,256]{2,1,0:T(8,128)(2,1)} %scatter_fusion), calls=%async_computation.1 | async-start | bytes 4194304 | tf_op jit(solution)/shard_map/all_to_all | solution.py:96
  32.9 74.3 %all-gather.13.cloned.1.call-start = ((), (), s32[]{:S(2)}) async-start(), calls=%async_computation.8 | async-start | bytes 4587520 | tf_op jit(solution)/shard_map/all_gather | solution.py:105
  63.1 98.9 %all-gather.9.cloned.1.call-start = ((), (), s32[]{:S(2)}) async-start(), calls=%async_computation.5 | async-start | bytes 6488064 | tf_op jit(solution)/shard_map/all_gather | solution.py:66
  64.0 181.7 %all-gather.11.cloned.1.call-start = ((), (), s32[]{:S(2)}) async-start(), calls=%async_computation.6 | async-start | bytes 2621440 | tf_op jit(solution)/shard_map/all_gather | solution.py:79
  195.8 8.7 %copy-start.6 = (bf16[1792,64]{0,1:T(8,128)(2,1)S(1)}, bf16[1792,64]{0,1:T(8,128)(2,1)}, u32[]{:S(2)}) copy-start(bf16[1792,64]{0,1:T(8,128)(2,1)} %get-tuple-element.361) | copy-start | bytes 688132
  216.3 23.1 %all-to-all-start.2 = ((bf16[14,4,32,256]{3,2,0,1:T(8,128)(2,1)}), bf16[14,4,32,256]{3,2,0,1:T(8,128)(2,1)S(1)}, u32[]{:S(2)}, u32[]{:S(2)}) async-start(bf16[14,4,32,256]{3,2,0,1:T(8,128)(2,1)} %copy.105), calls=%async_computation.2 | async-start | bytes 1835008 | tf_op jit(solution)/shard_map/all_to_all | solution.py:122
  220.2 78.7 %all-gather.15.cloned.1.call-start = ((), (), s32[]{:S(2)}) async-start(), calls=%async_computation.9 | async-start | bytes 4587520 | tf_op jit(solution)/shard_map/all_gather | solution.py:144
  220.2 32.4 %copy-start.8 = (f32[1024]{0:T(1024)S(1)}, f32[1024]{0:T(1024)}, u32[]{:S(2)}) copy-start(f32[1024]{0:T(1024)} %param.33) | copy-start | bytes 12292
  220.2 32.4 %copy-start.9 = (f32[1024]{0:T(1024)S(1)}, f32[1024]{0:T(1024)}, u32[]{:S(2)}) copy-start(f32[1024]{0:T(1024)} %param.32) | copy-start | bytes 12292
  254.0 118.7 %reduce-scatter.2.cloned.1.call-start = ((), (), s32[]{:S(2)}) async-start(), calls=%async_computation.7 | async-start | bytes 4587520 | tf_op jit(solution)/shard_map/reduce_scatter | solution.py:151
  329.6 46.8 %copy-start.16 = (f32[1024]{0:T(1024)S(1)}, f32[1024]{0:T(1024)}, u32[]{:S(2)}) copy-start(f32[1024]{0:T(1024)} %param.35) | copy-start | bytes 12292
  329.6 46.8 %copy-start.17 = (f32[1024]{0:T(1024)S(1)}, f32[1024]{0:T(1024)}, u32[]{:S(2)}) copy-start(f32[1024]{0:T(1024)} %param.34) | copy-start | bytes 12292
  379.2 13.0 %copy-start.19 = (s32[14]{0:T(128)S(1)}, s32[14]{0:T(128)}, u32[]{:S(2)}) copy-start(s32[14]{0:T(128)} %copy-done.18) | copy-start | bytes 172
  381.2 41.1 %copy-start.1 = (bf16[1792,256]{0,1:T(8,128)(2,1)S(1)}, bf16[1792,256]{0,1:T(8,128)(2,1)}, u32[]{:S(2)}) copy-start(bf16[1792,256]{0,1:T(8,128)(2,1)} %copy-done) | copy-start | bytes 2752516
  384.4 36.4 %all-to-all-start.3 = ((bf16[32,32,1024]{2,1,0:T(8,128)(2,1)}), bf16[32,32,1024]{2,1,0:T(8,128)(2,1)S(1)}, u32[]{:S(2)}, u32[]{:S(2)}) async-start(bf16[32,32,1024]{2,1,0:T(8,128)(2,1)} %broadcast_select_fusion), calls=%async_computation.4 | async-start | bytes 4194304 | tf_op jit(solution)/shard_map/all_to_all | solution.py:163
  392.2 70.7 %all-gather.17.cloned.1.call-start = ((), (), s32[]{:S(2)}) async-start(), calls=%async_computation.10 | async-start | bytes 4587520 | tf_op jit(solution)/shard_map/all_gather | solution.py:165
  (9 other events, 36.8 us)
Sparse Core Ops, SparseCore 0:
  63.2 43.9 all-gather.12
  110.0 51.8 all-gather.8
  206.8 38.8 all-gather.10
  254.1 44.7 all-gather.14
  329.7 42.8 reduce-scatter.1
  422.5 40.4 all-gather.16
where the time goes:
time: 480 us; the launch traced here: 474 us
  waiting for transfers between devices  304 us (63%)
  matrix products  64.6 us (13%)
  local copies, waits for them, and re-layouts  38.6 us (8%)
  starting transfers between devices  27.4 us (6%)
  other arithmetic  24 us (5%)
  between operations  15 us (3%)
    all_gather x1, waiting for transfers between devices, body(): gathered = lax.all_gather(local, 'dp', axis=0, tiled=True)  54.7 us
    all_gather x1, waiting for transfers between devices, body(): lax.all_gather(first_mine, 'mp', axis=1).reshape(pages_dev * page, width)  44.9 us
    reduce_scatter x1, waiting for transfers between devices, body(): lax.psum_scatter(fed_term.reshape(pages_dev, n_model, sub, width), 'mp',...  43 us
    all_gather x1, waiting for transfers between devices, body(): lax.all_gather(dealt_part, 'mp', axis=2, tiled=True)  42.6 us
    all_gather x1, waiting for transfers between devices, body(): lax.all_gather(mixed_mine, 'mp', axis=1).reshape(pages_dev * page, width)  35.7 us
    all_to_all x1, waiting for transfers between devices, body(): lax.all_to_all(outgoing, 'dp', split_axis=0, concat_axis=0, tiled=True)  28.5 us
    all_to_all x1, waiting for transfers between devices, body(): lax.all_to_all(send_pages, 'dp', split_axis=0, concat_axis=0, tiled=True)  27.3 us
    dot_general x1, matrix products, body(): jnp.einsum('tu,ou->to', hidden, down_t, preferred_element_type=jnp.float32)  26.1 us
  transfers between devices with their start and end apart: 10, of which 10 were waited for; matrix products, arithmetic and copies ran while one was open for 5% of the time, Pallas kernels for 0%

commit v1 on v0

--- a/solution.py
+++ b/solution.py
@@ -2,8 +2,25 @@
 import jax.numpy as jnp
 from jax import lax
 from jax.sharding import PartitionSpec as P
+from jax.lax import axis_index, axis_size, ppermute
 
 HEAD = 64
+
+
+def carry_the_page(shard_in, across):
+    chips = axis_size(across)
+    block_list = [(b, (b + 1) % chips) for b in range(chips)]
+    aux, built = ([shard_in], [shard_in])
+    trail = [(b, (b - 1) % chips) for b in range(chips)]
+    for _ in range(chips // 2):
+        aux.append(ppermute(aux[-1], axis_name=across, perm=block_list))
+    for _ in [*range((chips - 1) // 2)]:
+        built.append(ppermute(built[-1], axis_name=across, perm=trail))
+    return jnp.roll(
+        jnp.concatenate([*aux[::-1], *built[1:]], axis=2),
+        (axis_index(across) - chips // 2) * shard_in.shape[2],
+        axis=2,
+    )
 
 
 def layer_norm(hidden_sum, gain, shift):
@@ -102,7 +119,7 @@
         jnp.where(matches, jnp.arange(buffer_rows, dtype=jnp.int32)[None, :], 0), axis=1
     )
     dealt_part = got_pages[source_row]
-    dealt = lax.all_gather(dealt_part, "mp", axis=2, tiled=True).reshape(pages_dev * page, width)
+    dealt = carry_the_page(dealt_part, "mp").reshape(pages_dev * page, width)
     dealt_ids = got_ids[source_row].reshape(pages_dev * page)
     query = jnp.dot(dealt, full_query, preferred_element_type=jnp.float32).astype(jnp.bfloat16)
     keys = jnp.dot(dealt, full_key, preferred_element_type=jnp.float32).astype(jnp.bfloat16)

time: 480 us -> 451 us (0.940)
  waiting for transfers between devices: 304 us -> 258 us
  local copies, waits for them, and re-layouts: 38.6 us -> 48.5 us
    all_gather x1, waiting for transfers between devices: 54.7 us -> 0.01 us  [body(): gathered = lax.all_gather(local, 'dp', axis=0, tiled=True)]
    all_gather x1 -> x0, waiting for transfers between devices: 42.6 us -> none  [body(): lax.all_gather(dealt_part, 'mp', axis=2, tiled=True)]
    ppermute x0 -> x3, waiting for transfers between devices: none -> 37 us  [the longest x2 37 us: carry_the_page(): aux.append(ppermute(aux[-1], axis_name=across, perm=block_list))]
    all_to_all x1, waiting for transfers between devices: 27.3 us -> 36.4 us  [body(): lax.all_to_all(send_pages, 'dp', split_axis=0, concat_axis=0, tiled=True)]
    unnamed x54 -> x49, local copies, waits for them, and re-layouts: 11 us -> 17.8 us
    all_gather x1, waiting for transfers between devices: 6.34 us -> 11.6 us  [body(): out_all_t = lax.all_gather(out_t, 'mp', axis=1, tiled=True)]
  transfers between devices with their start and end apart: 10 -> 12, of which waited for: 10 -> 10; matrix products, arithmetic and copies ran while one was open for 5% -> 7% of each run, Pallas kernels for 0% -> 0%
where the time goes in v1:
time: 451 us; the launch traced here: 443 us
  waiting for transfers between devices  258 us (57%)
  matrix products  66.4 us (15%)
  local copies, waits for them, and re-layouts  48.5 us (11%)
  starting transfers between devices  30.9 us (7%)
  other arithmetic  24 us (5%)
  between operations  14.6 us (3%)
    all_gather x1, waiting for transfers between devices, body(): lax.all_gather(first_mine, 'mp', axis=1).reshape(pages_dev * page, width)  43.8 us
    reduce_scatter x1, waiting for transfers between devices, body(): lax.psum_scatter(fed_term.reshape(pages_dev, n_model, sub, width), 'mp',...  43 us
    ppermute x2, waiting for transfers between devices, carry_the_page(): aux.append(ppermute(aux[-1], axis_name=across, perm=block_list))  37 us
    all_to_all x1, waiting for transfers between devices, body(): lax.all_to_all(send_pages, 'dp', split_axis=0, concat_axis=0, tiled=True)  36.4 us
    all_gather x1, waiting for transfers between devices, body(): lax.all_gather(mixed_mine, 'mp', axis=1).reshape(pages_dev * page, width)  35.7 us
    all_to_all x1, waiting for transfers between devices, body(): lax.all_to_all(outgoing, 'dp', split_axis=0, concat_axis=0, tiled=True)  28.5 us
    dot_general x1, matrix products, body(): jnp.einsum('tu,ou->to', hidden, down_t, preferred_element_type=jnp.float32)  26.1 us
    all_to_all x1, waiting for transfers between devices, body(): lax.all_to_all(context.reshape(pages_dev, n_model, sub, head_cols), 'mp',...  20.2 us
  transfers between devices with their start and end apart: 12, of which 10 were waited for; matrix products, arithmetic and copies ran while one was open for 7% of the time, Pallas kernels for 0%

profile of v1, /device:TPU:1, one launch (start us, length us, event | category | flops | bytes accessed | tf_op | source)
XLA Modules:
  0.0 443.2 jit_solution(5221886848913191905)
XLA Ops:
  15.5 9.6 %all-to-all-start = ((s32[32,1,129]{2,1,0:T(1,128)}), s32[32,1,129]{2,1,0:T(1,128)S(1)}, u32[]{:S(2)}, u32[]{:S(2)}) async-start(s32[32,1,129]{2,1,0:T(1,128)} %all_to_all.17), calls=%async_computation | async-start | bytes 65536 | tf_op jit(solution)/shard_map/all_to_all | solution.py:114
  32.4 5.8 %all-to-all-start.1 = ((bf16[32,128,256]{2,1,0:T(8,128)(2,1)}), bf16[32,128,256]{2,1,0:T(8,128)(2,1)S(1)}, u32[]{:S(2)}, u32[]{:S(2)}) async-start(bf16[32,128,256]{2,1,0:T(8,128)(2,1)} %scatter_fusion), calls=%async_computation.1 | async-start | bytes 4194304 | tf_op jit(solution)/shard_map/all_to_all | solution.py:113
  39.5 36.4 %all-to-all-done.1 = bf16[32,128,256]{2,1,0:T(8,128)(2,1)S(1)} async-done(((bf16[32,128,256]{2,1,0:T(8,128)(2,1)}), bf16[32,128,256]{2,1,0:T(8,128)(2,1)S(1)}, u32[]{:S(2)}, u32[]{:S(2)}) %all-to-all-start.1) | async-done | bytes 2097184 | tf_op jit(solution)/shard_map/all_to_all | solution.py:113
  77.8 19.9 %collective-permute-done = bf16[14,128,256]{2,1,0:T(8,128)(2,1)S(1)} collective-permute-done((bf16[14,128,256]{2,1,0:T(8,128)(2,1)S(1)}, bf16[14,128,256]{2,1,0:T(8,128)(2,1)S(1)}, u32[]{:S(2)}, u32[]{:S(2)}) %collective-permute-start) | collective-permute-done | bytes 917536 | tf_op jit(solution)/shard_map/ppermute | solution.py:16
  101.0 17.1 %collective-permute-done.1 = bf16[14,128,256]{2,1,0:T(8,128)(2,1)} collective-permute-done((bf16[14,128,256]{2,1,0:T(8,128)(2,1)S(1)}, bf16[14,128,256]{2,1,0:T(8,128)(2,1)}, u32[]{:S(2)}, u32[]{:S(2)}) %collective-permute-start.1) | collective-permute-done | bytes 917536 | tf_op jit(solution)/shard_map/ppermute | solution.py:16
  123.7 3.3 convolution_convert_fusion.2
  129.0 3.3 convolution_convert_fusion.1
  134.3 3.3 convolution_convert_fusion.3
  138.6 8.2 %while.41 = (s32[]{:T(128)}, bf16[2,896,64]{1,2,0:T(8,128)(2,1)S(1)}, s32[2,896]{1,0:T(2,128)S(1)}, s32[14,128]{1,0:T(8,128)S(1)}, bf16[2,896,64]{2,1,0:T(8,128)...) while((s32[]{:T(128)}, bf16[2,896,64]{1,2,0:T(8,128)(2,1)S(1)}, ...), condition=%wide.region_7.8_spmd, body=%wide.region_4.7_spmd.sunk | while | flops 425548032 | bytes 20567648 | solution.py:50
  148.7 7.6 %while.42 = (s32[]{:T(128)}, bf16[2,896,64]{1,2,0:T(8,128)(2,1)S(1)}, s32[2,896]{1,0:T(2,128)S(1)}, s32[14,128]{1,0:T(8,128)S(1)}, bf16[2,896,64]{2,1,0:T(8,128)...) while((s32[]{:T(128)}, bf16[2,896,64]{1,2,0:T(8,128)(2,1)S(1)}, ...), condition=%wide.region_11.12_spmd, body=%wide.region_8.11_spmd.sunk | while | flops 425548032 | bytes 20567648 | solution.py:50
  157.5 7.8 %while.43 = (s32[]{:T(128)}, bf16[2,896,64]{1,2,0:T(8,128)(2,1)S(1)}, s32[2,896]{1,0:T(2,128)S(1)}, s32[14,128]{1,0:T(8,128)S(1)}, bf16[2,896,64]{2,1,0:T(8,128)...) while((s32[]{:T(128)}, bf16[2,896,64]{1,2,0:T(8,128)(2,1)S(1)}, ...), condition=%wide.region_15.16_spmd, body=%wide.region_12.15_spmd.sunk | while | flops 425548032 | bytes 20567648 | solution.py:50
  169.1 9.6 %while.44 = (s32[]{:T(128)}, bf16[2,896,64]{1,2,0:T(8,128)(2,1)S(1)}, s32[2,896]{1,0:T(2,128)S(1)}, s32[14,128]{1,0:T(8,128)S(1)}, bf16[2,896,64]{2,1,0:T(8,128)...) while((s32[]{:T(128)}, bf16[2,896,64]{1,2,0:T(8,128)(2,1)S(1)}, ...), condition=%wide.region_19.20_spmd, body=%wide.region_16.19_spmd.sunk | while | flops 425548032 | bytes 20337244 | solution.py:50
  180.6 3.5 all-to-all-start.2
  184.2 20.2 %all-to-all-done.2 = bf16[14,4,32,256]{3,2,0,1:T(8,128)(2,1)S(1)} async-done(((bf16[14,4,32,256]{3,2,0,1:T(8,128)(2,1)}), bf16[14,4,32,256]{3,2,0,1:T(8,128)(2,1)S(1)}, u32[]{:S(2)}, u32[]{:S(2)}) %all-to-all-start.2) | async-done | bytes 917536 | tf_op jit(solution)/shard_map/all_to_all | solution.py:139
  204.4 11.6 %all-gather.9.cloned.1.call-done = bf16[1024,1024]{1,0:T(8,128)(2,1)} async-done(((bf16[1024,256]{1,0:T(8,128)(2,1)}), bf16[1024,1024]{1,0:T(8,128)(2,1)}) %all-gather.9.cloned.1.call-update) | async-done | bytes 2097168 | tf_op jit(solution)/shard_map/all_gather | solution.py:96
  224.3 43.8 %all-gather.11.cloned.1.call-done = bf16[14,128,1024]{2,1,0:T(8,128)(2,1)} async-done(((bf16[14,32,1024]{2,1,0:T(8,128)(2,1)}), bf16[14,128,1024]{2,1,0:T(8,128)(2,1)}) %all-gather.11.cloned.1.call-update) | async-done | bytes 3670032 | tf_op jit(solution)/shard_map/all_gather | solution.py:161
  268.1 26.1 %convolution_convert_fusion = bf16[1792,1024]{1,0:T(8,128)(2,1)} fusion(bf16[1024,3072]{1,0:T(8,128)(2,1)} %all-gather.7.cloned.1.call-done, bf16[1792,1024]{1,0:T(8,128)(2,1)} %bitcast.186), kind=kOutput, calls=%fused_computation.73 | convolution fusion | flops 7637303296 | bytes 11534336 | tf_op jit(solution)/shard_map/tu,ou->to/dot_general | solution.py:165
  294.3 4.5 %copy.99 = bf16[14,4,32,1024]{3,2,0,1:T(8,128)(2,1)} copy(bf16[14,4,32,1024]{3,2,1,0:T(8,128)(2,1)} %bitcast.169) | data formatting | bytes 7340032 | tf_op jit(solution)/shard_map/reshape | solution.py:169
  298.8 43.0 %reduce-scatter.2.cloned.1.call-done = bf16[14,1,32,1024]{3,2,0,1:T(8,128)(2,1)} async-done(((bf16[14,4,32,1024]{3,2,0,1:T(8,128)(2,1)}), bf16[14,1,32,1024]{3,2,0,1:T(8,128)(2,1)}) %reduce-scatter.2.cloned.1.call-update) | async-done | bytes 917520 | tf_op jit(solution)/shard_map/reduce_scatter | solution.py:168
  353.7 7.8 %all-to-all-start.3 = ((bf16[32,32,1024]{2,1,0:T(8,128)(2,1)}), bf16[32,32,1024]{2,1,0:T(8,128)(2,1)S(1)}, u32[]{:S(2)}, u32[]{:S(2)}) async-start(bf16[32,32,1024]{2,1,0:T(8,128)(2,1)} %broadcast_select_fusion), calls=%async_computation.4 | async-start | bytes 4194304 | tf_op jit(solution)/shard_map/all_to_all | solution.py:180
  361.5 28.5 %all-to-all-done.3 = bf16[32,32,1024]{2,1,0:T(8,128)(2,1)S(1)} async-done(((bf16[32,32,1024]{2,1,0:T(8,128)(2,1)}), bf16[32,32,1024]{2,1,0:T(8,128)(2,1)S(1)}, u32[]{:S(2)}, u32[]{:S(2)}) %all-to-all-start.3) | async-done | bytes 2097184 | tf_op jit(solution)/shard_map/all_to_all | solution.py:180
  393.0 3.6 copy.100
  396.5 35.7 %all-gather.13.cloned.1.call-done = bf16[14,128,1024]{2,1,0:T(8,128)(2,1)} async-done(((bf16[14,32,1024]{2,1,0:T(8,128)(2,1)}), bf16[14,128,1024]{2,1,0:T(8,128)(2,1)}) %all-gather.13.cloned.1.call-update) | async-done | bytes 3670032 | tf_op jit(solution)/shard_map/all_gather | solution.py:182
  432.2 4.2 copy.153
  (162 shorter events, 96.5 us)
Async XLA Ops:
  7.2 116.6 %all-gather.7.cloned.1.call-start = ((), (), s32[]{:S(2)}) async-start(), calls=%async_computation.5 | async-start | bytes 6488064 | tf_op jit(solution)/shard_map/all_gather | solution.py:83
  13.3 19.0 %copy-start.12 = (s32[14]{0:T(128)}, s32[14]{0:T(128)S(1)}, u32[]{:S(2)}) copy-start(s32[14]{0:T(128)S(1)} %compare_select_fusion.2) | copy-start | bytes 172
  15.5 16.9 %all-to-all-start = ((s32[32,1,129]{2,1,0:T(1,128)}), s32[32,1,129]{2,1,0:T(1,128)S(1)}, u32[]{:S(2)}, u32[]{:S(2)}) async-start(s32[32,1,129]{2,1,0:T(1,128)} %all_to_all.17), calls=%async_computation | async-start | bytes 65536 | tf_op jit(solution)/shard_map/all_to_all | solution.py:114
  32.4 43.5 %all-to-all-start.1 = ((bf16[32,128,256]{2,1,0:T(8,128)(2,1)}), bf16[32,128,256]{2,1,0:T(8,128)(2,1)S(1)}, u32[]{:S(2)}, u32[]{:S(2)}) async-start(bf16[32,128,256]{2,1,0:T(8,128)(2,1)} %scatter_fusion), calls=%async_computation.1 | async-start | bytes 4194304 | tf_op jit(solution)/shard_map/all_to_all | solution.py:113
  38.2 177.8 %all-gather.9.cloned.1.call-start = ((), (), s32[]{:S(2)}) async-start(), calls=%async_computation.6 | async-start | bytes 2621440 | tf_op jit(solution)/shard_map/all_gather | solution.py:96
  76.5 21.2 %collective-permute-start = (bf16[14,128,256]{2,1,0:T(8,128)(2,1)S(1)}, bf16[14,128,256]{2,1,0:T(8,128)(2,1)S(1)}, u32[]{:S(2)}, u32[]{:S(2)}) collective-permute-start(bf16[14,128,256]{2,1,0:T(8,128)(2,1)S(1)} %gather_fusion), channel_id=1, source_target_pairs={{0,1},{1,2},{2,3},{3,0},{4,5},{5,6},{6,7},{7,4},{8,9},{9,10},{10,1... | collective-permute-start | bytes 2752520 | tf_op jit(solution)/shard_map/ppermute | solution.py:16
  97.7 20.4 %collective-permute-start.1 = (bf16[14,128,256]{2,1,0:T(8,128)(2,1)S(1)}, bf16[14,128,256]{2,1,0:T(8,128)(2,1)}, u32[]{:S(2)}, u32[]{:S(2)}) collective-permute-start(bf16[14,128,256]{2,1,0:T(8,128)(2,1)S(1)} %collective-permute-done), channel_id=1, source_target_pairs={{0,1},{1,2},{2,3},{3,0},{4,5},{5,6},{6,7},{7,4},{8,9},{9,10},{10,1... | collective-permute-start | bytes 2752520 | tf_op jit(solution)/shard_map/ppermute | solution.py:16
  97.7 21.9 %collective-permute-start.2 = (bf16[14,128,256]{2,1,0:T(8,128)(2,1)S(1)}, bf16[14,128,256]{2,1,0:T(8,128)(2,1)S(1)}, u32[]{:S(2)}, u32[]{:S(2)}) collective-permute-start(bf16[14,128,256]{2,1,0:T(8,128)(2,1)S(1)} %gather_fusion), channel_id=1, source_target_pairs={{0,3},{1,0},{2,1},{3,2},{4,7},{5,4},{6,5},{7,6},{8,11},{9,8},{10,9... | collective-permute-start | bytes 2752520 | tf_op jit(solution)/shard_map/ppermute | solution.py:18
  157.5 8.1 %copy-start.4 = (bf16[1792,64]{0,1:T(8,128)(2,1)S(1)}, bf16[1792,64]{0,1:T(8,128)(2,1)}, u32[]{:S(2)}) copy-start(bf16[1792,64]{0,1:T(8,128)(2,1)} %get-tuple-element.357) | copy-start | bytes 688132
  157.5 8.4 %copy-start.5 = (bf16[1792,64]{0,1:T(8,128)(2,1)S(1)}, bf16[1792,64]{0,1:T(8,128)(2,1)}, u32[]{:S(2)}) copy-start(bf16[1792,64]{0,1:T(8,128)(2,1)} %get-tuple-element.353) | copy-start | bytes 688132
  157.5 8.7 %copy-start.6 = (bf16[1792,64]{0,1:T(8,128)(2,1)S(1)}, bf16[1792,64]{0,1:T(8,128)(2,1)}, u32[]{:S(2)}) copy-start(bf16[1792,64]{0,1:T(8,128)(2,1)} %get-tuple-element.361) | copy-start | bytes 688132
  169.1 9.9 %copy-start.3 = (bf16[2,896,64]{2,1,0:T(8,128)(2,1)S(1)}, bf16[2,896,64]{2,1,0:T(8,128)(2,1)}, u32[]{:S(2)}) copy-start(bf16[2,896,64]{2,1,0:T(8,128)(2,1)} %copy.82) | copy-start | bytes 688132
  180.6 23.8 %all-to-all-start.2 = ((bf16[14,4,32,256]{3,2,0,1:T(8,128)(2,1)}), bf16[14,4,32,256]{3,2,0,1:T(8,128)(2,1)S(1)}, u32[]{:S(2)}, u32[]{:S(2)}) async-start(bf16[14,4,32,256]{3,2,0,1:T(8,128)(2,1)} %copy.105), calls=%async_computation.2 | async-start | bytes 1835008 | tf_op jit(solution)/shard_map/all_to_all | solution.py:139
  184.1 84.0 %all-gather.11.cloned.1.call-start = ((), (), s32[]{:S(2)}) async-start(), calls=%async_computation.8 | async-start | bytes 4587520 | tf_op jit(solution)/shard_map/all_gather | solution.py:161
  184.2 38.7 %copy-start.8 = (f32[1024]{0:T(1024)S(1)}, f32[1024]{0:T(1024)}, u32[]{:S(2)}) copy-start(f32[1024]{0:T(1024)} %param.33) | copy-start | bytes 12292
  184.2 38.7 %copy-start.9 = (f32[1024]{0:T(1024)S(1)}, f32[1024]{0:T(1024)}, u32[]{:S(2)}) copy-start(f32[1024]{0:T(1024)} %param.32) | copy-start | bytes 12292
  224.2 117.6 %reduce-scatter.2.cloned.1.call-start = ((), (), s32[]{:S(2)}) async-start(), calls=%async_computation.7 | async-start | bytes 4587520 | tf_op jit(solution)/shard_map/reduce_scatter | solution.py:168
  294.2 4.6 %copy-start.16 = (s32[32]{0:T(128)S(1)}, s32[32]{0:T(128)}, u32[]{:S(2)}) copy-start(s32[32]{0:T(128)} %copy-done.15) | copy-start | bytes 388
  298.8 46.8 %copy-start.10 = (f32[1024]{0:T(1024)S(1)}, f32[1024]{0:T(1024)}, u32[]{:S(2)}) copy-start(f32[1024]{0:T(1024)} %param.35) | copy-start | bytes 12292
  298.8 46.8 %copy-start.11 = (f32[1024]{0:T(1024)S(1)}, f32[1024]{0:T(1024)}, u32[]{:S(2)}) copy-start(f32[1024]{0:T(1024)} %param.34) | copy-start | bytes 12292
  348.4 13.1 %copy-start.13 = (s32[14]{0:T(128)S(1)}, s32[14]{0:T(128)}, u32[]{:S(2)}) copy-start(s32[14]{0:T(128)} %copy-done.12) | copy-start | bytes 172
  350.5 41.1 %copy-start.1 = (bf16[1792,256]{0,1:T(8,128)(2,1)S(1)}, bf16[1792,256]{0,1:T(8,128)(2,1)}, u32[]{:S(2)}) copy-start(bf16[1792,256]{0,1:T(8,128)(2,1)} %copy-done) | copy-start | bytes 2752516
  353.7 36.4 %all-to-all-start.3 = ((bf16[32,32,1024]{2,1,0:T(8,128)(2,1)}), bf16[32,32,1024]{2,1,0:T(8,128)(2,1)S(1)}, u32[]{:S(2)}, u32[]{:S(2)}) async-start(bf16[32,32,1024]{2,1,0:T(8,128)(2,1)} %broadcast_select_fusion), calls=%async_computation.4 | async-start | bytes 4194304 | tf_op jit(solution)/shard_map/all_to_all | solution.py:180
  361.4 70.7 %all-gather.13.cloned.1.call-start = ((), (), s32[]{:S(2)}) async-start(), calls=%async_computation.9 | async-start | bytes 4587520 | tf_op jit(solution)/shard_map/all_gather | solution.py:182
  (5 other events, 7.7 us)
Sparse Core Ops, SparseCore 0:
  12.6 66.4 all-gather.6
  169.2 46.6 all-gather.8
  224.4 43.7 all-gather.10
  298.9 42.8 reduce-scatter.1
  391.7 40.4 all-gather.12
